TPU v7x, 512 devices: a whole 4x8x8 slice. The times are simulated.
512 devices in a mesh: call: 8 (over z), tm: 64 (over x, y, core).
Axes of the slice: x: 4, y: 8, z: 8, core: 2. Of those that a mesh axis runs over, the one named last changes fastest.
Arguments:
- frames: bfloat16 [8, 8192, 1024], P('call', 'tm'), may hold values from -6 to 6
- lengths: int32 [8], replicated, may hold values from 2048 to 8192, as said below
- ln_attn_gain: float32 [1024], replicated, may hold values from 0.5 to 1.5
- w_qkv: bfloat16 [1024, 3072], P('tm'), may hold values from -0.1875 to 0.1875
- w_out: bfloat16 [1024, 1024], P('tm'), may hold values from -1.5 to 1.5
- ln_conv_gain: float32 [1024], replicated, may hold values from 0.5 to 1.5
- w_pw1: bfloat16 [1024, 2048], P('tm'), may hold values from -0.1875 to 0.1875
- dw_kernel: float32 [9, 1024], replicated, may hold values from -2 to 2
- bn_gain: float32 [1024], replicated, may hold values from 0.5 to 1.5
- bn_bias: float32 [1024], replicated, may hold values from -3 to 3
Outputs:
- attended: bfloat16 [8, 8192, 1024], P('call', 'tm')
- conv_act: bfloat16 [8, 8192, 1024], P('call', 'tm')
Inputs may be any that keep to these rules, and one draw needn't show every extreme that they name: `lengths`: valid frames of each call; at least one call of the batch fills all 8192 frames.
All inputs are finite; a program needn't handle non-finite values.
Results may differ from a plain program's by a relative error of at most 0.009.
Values may be sent and summed in bfloat16 or wider, within the bound.
No kernel may reach another device: no remote copies, remote signals or barrier semaphores. Data moves between devices by JAX's collectives and lax.ppermute only.
A program may use at most 64 MiB of HBM per device.

v0:
```python
import jax
import jax.numpy as jnp
import numpy as np
from jax import lax
from jax.sharding import Mesh
from jax.sharding import PartitionSpec as P

HEAD_DIM = 64
SPAN = 128
LEFT = 1024
KERNEL = 9
TM = ("x", "y", "core")


def passed_along(value, axis, steps):
    count = lax.axis_size(axis)
    first, last = (max(0, -steps), min(count, count - steps))
    return lax.ppermute(value, axis, [(source, source + steps) for source in range(first, last)])


def with_halo(cells, axis, width):
    count = lax.axis_size(axis)
    ends = count - 1
    head = lax.slice_in_dim(cells, 0, width, axis=0)
    tail = lax.slice_in_dim(cells, cells.shape[0] - width, cells.shape[0], axis=0)
    return jnp.concatenate(
        [
            lax.ppermute(tail, axis, [(i, (i + 1) % count) for i in range(ends)]),
            cells,
            lax.ppermute(head, axis, [((i + 1) % count, i) for i in range(ends)]),
        ],
        axis=0,
    )


def layer_norm(values, gain_vec):
    wide = values.astype(jnp.float32)
    center = wide - jnp.mean(wide, axis=-1, keepdims=True)
    spread = jnp.mean(center * center, axis=-1, keepdims=True)
    return center * lax.rsqrt(spread + 1e-05) * gain_vec


def contract_with(left, rows_piece):
    return jnp.dot(left, rows_piece, preferred_element_type=jnp.float32)


def on_device(
    frames, lengths, ln_attn_gain, w_qkv, w_out, ln_conv_gain, w_pw1, dw_kernel, bn_gain, bn_bias
):
    stream = frames[0]
    frame_count, model_width = stream.shape
    head_count = model_width // HEAD_DIM
    length = lax.dynamic_index_in_dim(lengths, lax.axis_index("call"), 0, keepdims=False)
    first_row = lax.axis_index(TM) * frame_count
    query_pos = first_row + jnp.arange(frame_count, dtype=jnp.int32)
    frame_valid = query_pos < length
    qkv_cols = w_qkv.shape[1]
    out_cols = w_out.shape[1]
    core = lax.axis_index("core")
    cores = lax.axis_size("core")
    swap = [(0, 1), (1, 0)]
    packed = jnp.concatenate([w_qkv, w_out, w_pw1], axis=1)
    half = packed.shape[1] // 2
    halves = (packed[:, :half], packed[:, half:])
    given = lax.ppermute(jnp.where(core == 0, halves[1], halves[0]), "core", swap)
    kept = jnp.where(core == 0, halves[0], halves[1])
    pair = jnp.where(core == 0, jnp.stack([kept, given]), jnp.stack([given, kept]))
    gathered = lax.all_gather(pair.reshape(-1, half), ("x", "y"), axis=0, tiled=True)
    prior_blocks = LEFT // frame_count
    chip_hops = prior_blocks // cores
    blocks = [stream]
    current = stream
    for hop_index in range(chip_hops):
        current = passed_along(current, ("x", "y"), 1)
        blocks.append(current)
    mine = jnp.stack(blocks[::-1])
    gathered, mine = lax.optimization_barrier((gathered, mine))
    other = lax.ppermute(gathered, "core", swap)
    weights = jnp.where(
        core == 0,
        jnp.concatenate([gathered, other], axis=1),
        jnp.concatenate([other, gathered], axis=1),
    )
    theirs = lax.ppermute(mine, "core", swap)
    by_chip = jnp.where(core == 0, jnp.stack([mine, theirs], 1), jnp.stack([theirs, mine], 1))
    by_chip = by_chip.reshape(-1, model_width)
    context_frames = lax.dynamic_slice_in_dim(
        by_chip, core * frame_count, (prior_blocks + 1) * frame_count, 0
    )
    key_count = context_frames.shape[0]
    normed_all = layer_norm(context_frames, ln_attn_gain).astype(jnp.bfloat16)
    normed = normed_all[key_count - frame_count :]
    queries = contract_with(normed, weights[:, :model_width]).astype(jnp.bfloat16)
    key_value = contract_with(normed_all, weights[:, model_width:qkv_cols])
    keys = key_value[:, :model_width].astype(jnp.bfloat16)
    values = key_value[:, model_width:].astype(jnp.bfloat16)
    key_pos = first_row - prior_blocks * frame_count + jnp.arange(key_count, dtype=jnp.int32)
    span_first = query_pos // SPAN * SPAN
    allowed = (key_pos[None, :] >= 0) & (key_pos[None, :] >= span_first[:, None] - LEFT)
    allowed = allowed & (key_pos[None, :] < span_first[:, None] + SPAN)
    allowed = allowed & ((key_pos[None, :] < length) | (key_pos[None, :] == query_pos[:, None]))
    group_size = 4
    group_count = head_count // group_size
    query_groups = queries.reshape(frame_count, group_count, group_size, HEAD_DIM).transpose(
        1, 0, 2, 3
    )
    key_groups = keys.reshape(key_count, group_count, group_size, HEAD_DIM).transpose(1, 0, 2, 3)
    value_groups = values.reshape(key_count, group_count, group_size, HEAD_DIM).transpose(
        1, 0, 2, 3
    )
    scale_factor = 1.0 / jnp.sqrt(jnp.float32(HEAD_DIM))

    def attend_group(operands):
        query_part, key_part, value_part = operands
        scores = (
            jnp.einsum("qhd,khd->hqk", query_part, key_part, preferred_element_type=jnp.float32)
            * scale_factor
        )
        raised = jnp.where(allowed[None], jnp.exp(scores), 0.0)
        probs = (raised / jnp.sum(raised, axis=-1, keepdims=True)).astype(jnp.bfloat16)
        mixed = jnp.einsum("hqk,khd->qhd", probs, value_part, preferred_element_type=jnp.float32)
        return mixed.astype(jnp.bfloat16)

    context = lax.map(attend_group, (query_groups, key_groups, value_groups))
    context = context.transpose(1, 0, 2, 3).reshape(frame_count, model_width)
    projected = contract_with(context, weights[:, qkv_cols : qkv_cols + out_cols])
    attended = jnp.where(frame_valid[:, None], stream.astype(jnp.float32) + projected, 0.0).astype(
        jnp.bfloat16
    )
    conv_in = layer_norm(attended, ln_conv_gain).astype(jnp.bfloat16)
    expanded = contract_with(conv_in, weights[:, qkv_cols + out_cols :])
    gated = expanded[:, :model_width] * jax.nn.sigmoid(expanded[:, model_width:])
    gated = jnp.where(frame_valid[:, None], gated, 0.0).astype(jnp.bfloat16)
    padded = with_halo(gated, TM, KERNEL // 2)
    depthwise = jnp.zeros((frame_count, model_width), jnp.float32)
    for tap_index in range(KERNEL):
        depthwise = (
            depthwise
            + padded[tap_index : tap_index + frame_count].astype(jnp.float32) * dw_kernel[tap_index]
        )
    masked = jnp.where(frame_valid[:, None], depthwise, 0.0)
    moments = (jnp.sum(masked, axis=0), jnp.sum(masked * depthwise, axis=0))
    for axis in ("core", "y", "x", "call"):
        moments = lax.psum(moments, axis)
    first_moment, second_moment = moments
    count_all = jnp.sum(lengths).astype(jnp.float32)
    average = first_moment / count_all
    second = second_moment / count_all
    normal_act = (depthwise - average) * lax.rsqrt(
        second - average * average + 1e-05
    ) * bn_gain + bn_bias
    activated = normal_act * jax.nn.sigmoid(normal_act)
    conv_act = jnp.where(frame_valid[:, None], activated, 0.0).astype(jnp.bfloat16)
    return (attended[None], conv_act[None])


def physical_mesh(mesh):
    devices = mesh.devices
    calls, tms = devices.shape
    first = devices[0]
    xs = len({d.coords[0] for d in first})
    ys = len({d.coords[1] for d in first})
    cores = tms // (xs * ys)
    grid = np.array([[(d.coords[0], d.coords[1], d.core_on_chip) for d in row] for row in devices])
    expect = np.stack(
        np.meshgrid(np.arange(xs), np.arange(ys), np.arange(cores), indexing="ij"), -1
    ).reshape(-1, 3)
    grid = grid - grid[:, :1]
    assert (grid == expect[None]).all()
    return Mesh(devices.reshape(calls, xs, ys, cores), ("call",) + TM)


def solution(mesh):
    mesh4 = physical_mesh(mesh)
    rows = P(TM, None)
    stream = P("call", TM, None)
    return jax.shard_map(
        on_device,
        mesh=mesh4,
        in_specs=(stream, P(), P(), rows, rows, P(), rows, P(), P(), P()),
        out_specs=(stream, stream),
        check_vma=False,
    )
```

profile of v0, /device:TPU:2, one launch (start us, length us, event | category | flops | bytes accessed | tf_op | source)
XLA Modules:
  0.0 247.2 jit_solution(3414614098629872642)
XLA Ops:
  7.2 0.0 copy-start.1
  7.2 0.0 all-gather.2.cloned.1.call-start
  7.2 0.8 constant_dynamic-update-slice_fusion.1
  8.0 0.8 constant_dynamic-update-slice_fusion
  8.9 0.9 select_bitcast_fusion
  9.8 1.9 collective-permute-start
  11.7 1.3 collective-permute-done
  13.0 0.7 maximum_select_fusion.2
  13.7 0.0 all-gather.2.cloned.1.call-update
  13.7 3.5 %collective-permute-start.1 = (bf16[128,1024]{1,0:T(8,128)(2,1)}, bf16[128,1024]{1,0:T(8,128)(2,1)S(1)}, u32[]{:S(2)}, u32[]{:S(2)}) collective-permute-start(bf16[128,1024]{1,0:T(8,128)(2,1)} %bitcast.81), channel_id=1, source_target_pairs={{0,2},{2,4},{4,6},{6,8},{8,10},{10,12},{12,14},{14,16},{16,18},{18... | collective-permute-start | bytes 786440 | tf_op jit(solution)/shard_map/ppermute | solution.py:18
  17.2 9.1 %collective-permute-done.1 = bf16[128,1024]{1,0:T(8,128)(2,1)S(1)} collective-permute-done((bf16[128,1024]{1,0:T(8,128)(2,1)}, bf16[128,1024]{1,0:T(8,128)(2,1)S(1)}, u32[]{:S(2)}, u32[]{:S(2)}) %collective-permute-start.1) | collective-permute-done | bytes 262176 | tf_op jit(solution)/shard_map/ppermute | solution.py:18
  26.3 1.9 collective-permute-start.2
  28.2 9.7 %collective-permute-done.2 = bf16[128,1024]{1,0:T(8,128)(2,1)S(1)} collective-permute-done((bf16[128,1024]{1,0:T(8,128)(2,1)S(1)}, bf16[128,1024]{1,0:T(8,128)(2,1)S(1)}, u32[]{:S(2)}, u32[]{:S(2)}) %collective-permute-start.2) | collective-permute-done | bytes 262176 | tf_op jit(solution)/shard_map/ppermute | solution.py:18
  37.9 1.9 collective-permute-start.3
  39.8 11.6 %collective-permute-done.3 = bf16[128,1024]{1,0:T(8,128)(2,1)S(1)} collective-permute-done((bf16[128,1024]{1,0:T(8,128)(2,1)S(1)}, bf16[128,1024]{1,0:T(8,128)(2,1)S(1)}, u32[]{:S(2)}, u32[]{:S(2)}) %collective-permute-start.3) | collective-permute-done | bytes 262176 | tf_op jit(solution)/shard_map/ppermute | solution.py:18
  51.4 1.9 collective-permute-start.4
  53.3 9.2 %collective-permute-done.4 = bf16[128,1024]{1,0:T(8,128)(2,1)S(1)} collective-permute-done((bf16[128,1024]{1,0:T(8,128)(2,1)S(1)}, bf16[128,1024]{1,0:T(8,128)(2,1)S(1)}, u32[]{:S(2)}, u32[]{:S(2)}) %collective-permute-start.4) | collective-permute-done | bytes 262176 | tf_op jit(solution)/shard_map/ppermute | solution.py:18
  62.6 48.2 %all-gather.2.cloned.1.call-done = bf16[1024,3072]{1,0:T(8,128)(2,1)} async-done(((bf16[32,3072]{1,0:T(8,128)(2,1)}), bf16[1024,3072]{1,0:T(8,128)(2,1)}) %all-gather.2.cloned.1.call-update) | async-done | bytes 6291472 | tf_op jit(solution)/shard_map/all_gather | solution.py:68
  110.9 1.9 collective-permute-start.6
  112.8 2.4 collective-permute-start.5
  115.2 0.6 dynamic_slice.18
  115.8 0.7 broadcast_compare_fusion
  116.5 0.7 fusion.66
  117.2 7.8 %collective-permute-done.5 = bf16[5,128,1024]{2,1,0:T(8,128)(2,1)S(1)} collective-permute-done((bf16[5,128,1024]{2,1,0:T(8,128)(2,1)S(1)}, bf16[5,128,1024]{2,1,0:T(8,128)(2,1)S(1)}, u32[]{:S(2)}, u32[]{:S(2)}) %collective-permute-start.5) | collective-permute-done | bytes 1310752 | tf_op jit(solution)/shard_map/ppermute | solution.py:84
  125.0 0.4 maximum_select_fusion.1
  125.4 0.2 copy.15
  125.7 0.4 convert_reduce_fusion
  126.1 0.8 fusion.20
  126.9 0.8 fusion.22
  127.7 0.7 slice-done.1
  128.4 10.2 %maximum_select_fusion = bf16[1024,6144]{1,0:T(8,128)(2,1)S(1)} fusion(bf16[1024,3072]{1,0:T(8,128)(2,1)} %collective-permute-done.6, bf16[1024,3072]{1,0:T(8,128)(2,1)S(1)} %bitcast.75, pred[]{:T(512)S(6)} %eq.6), kind=kLoop, calls=%fused_computation.20 | loop fusion | flops 56623104 | bytes 25165824 | tf_op jit(solution)/shard_map/jit(_where)/select_n | solution.py:79
  138.6 0.4 fusion.39
  139.0 4.1 %copy-done = bf16[1024,6144]{1,0:T(8,128)(2,1)} copy-done((bf16[1024,6144]{1,0:T(8,128)(2,1)}, bf16[1024,6144]{1,0:T(8,128)(2,1)S(1)}, u32[]{:S(2)}) %copy-start) | copy-done | bytes 12582936
  143.1 6.7 %convolution_convert_fusion = bf16[1152,2048]{1,0:T(8,128)(2,1)} fusion(bf16[1152,1024]{1,0:T(8,128)(2,1)S(1)} %fusion.22, bf16[1024,6144]{1,0:T(8,128)(2,1)S(1)} %maximum_select_fusion), kind=kOutput, calls=%fused_computation.21 | convolution fusion | flops 4834197504 | bytes 11272192 | tf_op jit(solution)/shard_map/dot_general | solution.py:44
  149.8 0.2 copy.17
  150.0 4.3 %fusion.69 = (bf16[1152,1024]{1,0:T(8,128)(2,1)S(1)}, bf16[1152,1024]{1,0:T(8,128)(2,1)}) fusion(bf16[1152,2048]{1,0:T(8,128)(2,1)} %convolution_convert_fusion), kind=kLoop, calls=%fused_computation.109 | loop fusion | bytes 9437184 | tf_op jit(solution)/shard_map/slice | solution.py:95
  154.3 4.3 %copy.16 = bf16[1152,1024]{0,1:T(8,128)(2,1)} copy(bf16[1152,1024]{1,0:T(8,128)(2,1)} %get-tuple-element.103) | data formatting | bytes 4718592 | tf_op jit(solution)/shard_map/slice | solution.py:96
  158.6 2.6 %copy.18 = bf16[1152,1024]{0,1:T(8,128)(2,1)} copy(bf16[1152,1024]{1,0:T(8,128)(2,1)S(1)} %get-tuple-element.102) | data formatting | bytes 4718592 | tf_op jit(solution)/shard_map/slice | solution.py:95
  161.2 15.3 %while.11 = (s32[]{:T(128)}, bf16[4,128,4,64]{1,3,2,0:T(8,128)(2,1)S(1)}, bf16[4,1152,4,64]{1,3,2,0:T(8,128)(2,1)}, bf16[4,128,4,64]{1,3,2,0:T(8,128)(2,1)S(1)},...) while((s32[]{:T(128)}, ...), condition=%wide.region_4.5_spmd.clone, body=%wide.region_2.4_spmd.clone.sunk | while | flops 154420864 | bytes 8694133 | solution.py:124
  161.2 0.3 or_and_fusion.2
  161.5 1.7 fusion.85
  163.2 1.8 fusion.86
  165.0 0.3 or_and_fusion.2
  165.3 1.7 fusion.85
  167.1 1.8 fusion.86
  168.8 0.3 or_and_fusion.2
  169.1 1.7 fusion.85
  170.9 1.7 fusion.86
  172.6 0.3 or_and_fusion.2
  172.9 1.7 fusion.85
  174.7 1.8 fusion.86
  176.5 2.2 convert_reduce_fusion.1
  178.6 0.2 fusion.44
  178.9 3.0 %fusion.23 = f32[128,2048]{1,0:T(8,128)S(1)} fusion(bf16[1024,6144]{1,0:T(8,128)(2,1)} %copy-done, bf16[128,1024]{1,0:T(8,128)(2,1)S(1)} %get-tuple-element.120, f32[1024]{0:T(1024)S(1)} %copy-done.7, f32[128]{0:T(128)S(1)} %add_rsqrt_fusion.2, f32[128]{0:T(128)S(1)} %broadcast_multiply_fusion.1), kind=kOutput, calls=%fused_computation.29 | convolution fusion | flops 537526272 | bytes 5510144 | tf_op jit(solution)/shard_map/dot_general | solution.py:44
  181.9 0.2 fusion.53
  182.1 2.0 collective-permute-start.7
  184.2 5.6 %collective-permute-start.8 = (bf16[4,1024]{1,0:T(4,128)(2,1)S(1)}, bf16[4,1024]{1,0:T(4,128)(2,1)S(1)}, u32[]{:S(2)}, u32[]{:S(2)}) collective-permute-start(bf16[4,1024]{1,0:T(4,128)(2,1)S(1)} %get-tuple-element.105), channel_id=1, source_target_pairs={{1,0},{2,1},{3,2},{4,3},{5,4},{6,5},{7,6},{8,7},{9,8},{10,9},{11,1... | collective-permute-start | bytes 24584 | tf_op jit(solution)/shard_map/ppermute | solution.py:30
  189.9 0.6 reduce_sum.77
  191.2 0.7 select_reduce_fusion
  191.8 2.5 %all-reduce.3 = (f32[1024]{0:T(1024)S(1)}, f32[1024]{0:T(1024)S(1)}) all-reduce(f32[1024]{0:T(1024)S(1)} %get-tuple-element.70, f32[1024]{0:T(1024)S(1)} %get-tuple-element.69), channel_id=1, replica_groups=mesh['call'=8,'x'=4,'y'=8,'core'=2] {'core'}, use_global_device_ids=true, to_apply=%region_14.15 | all-reduce | flops 2048 | bytes 16384 | tf_op jit(solution)/shard_map/psum | solution.py:144
  194.3 18.0 %all-reduce = (f32[1024]{0:T(1024)S(1)}, f32[1024]{0:T(1024)S(1)}) all-reduce(f32[1024]{0:T(1024)S(1)} %get-tuple-element.99, f32[1024]{0:T(1024)S(1)} %get-tuple-element.100), channel_id=1, replica_groups=mesh['call'=8,'x'=4,'y'=8,'core'=2] {'y'}, use_global_device_ids=true, to_apply=%region_15.16 | all-reduce | flops 2048 | bytes 16384 | tf_op jit(solution)/shard_map/psum | solution.py:144
  212.3 8.7 %all-reduce.2 = (f32[1024]{0:T(1024)S(1)}, f32[1024]{0:T(1024)S(1)}) all-reduce(f32[1024]{0:T(1024)S(1)} %get-tuple-element.93, f32[1024]{0:T(1024)S(1)} %get-tuple-element.94), channel_id=1, replica_groups=mesh['call'=8,'x'=4,'y'=8,'core'=2] {'x'}, use_global_device_ids=true, to_apply=%region_16.17 | all-reduce | flops 2048 | bytes 16384 | tf_op jit(solution)/shard_map/psum | solution.py:144
  221.0 18.4 %all-reduce.1 = (f32[1024]{0:T(1024)S(1)}, f32[1024]{0:T(1024)S(1)}) all-reduce(f32[1024]{0:T(1024)S(1)} %get-tuple-element.97, f32[1024]{0:T(1024)S(1)} %get-tuple-element.98), channel_id=1, replica_groups=mesh['call'=8,'x'=4,'y'=8,'core'=2] {'call'}, use_global_device_ids=true, to_apply=%region_17.18 | all-reduce | flops 2048 | bytes 16384 | tf_op jit(solution)/shard_map/psum | solution.py:144
  239.4 0.9 fusion.65
  (39 shorter events, 0.3 us)
Async XLA Ops:
  7.2 55.4 %copy-start.1 = (bf16[1,128,1024]{2,1,0:T(8,128)(2,1)S(1)}, bf16[1,128,1024]{2,1,0:T(8,128)(2,1)}, u32[]{:S(2)}) copy-start(bf16[1,128,1024]{2,1,0:T(8,128)(2,1)} %param.12) | copy-start | bytes 786436
  7.2 108.0 %copy-start.8 = (s32[8]{0:T(128)S(1)}, s32[8]{0:T(128)}, u32[]{:S(2)}) copy-start(s32[8]{0:T(128)} %param.13) | copy-start | bytes 100
  7.2 103.7 %all-gather.2.cloned.1.call-start = ((), (), s32[]{:S(2)}) async-start(), calls=%async_computation | async-start | bytes 6488064 | tf_op jit(solution)/shard_map/all_gather | solution.py:68
  9.8 3.2 %collective-permute-start = (bf16[16,3072]{1,0:T(8,128)(2,1)S(1)}, bf16[16,3072]{1,0:T(8,128)(2,1)S(1)}, u32[]{:S(2)}, u32[]{:S(2)}) collective-permute-start(bf16[16,3072]{1,0:T(8,128)(2,1)S(1)} %get-tuple-element.107), channel_id=1, source_target_pairs={{0,1},{1,0},{2,3},{3,2},{4,5},{5,4},{6,7},{7,6},{8,9},{9,8},{10,11... | collective-permute-start | bytes 294920 | tf_op jit(solution)/shard_map/ppermute | solution.py:65
  13.7 12.6 %collective-permute-start.1 = (bf16[128,1024]{1,0:T(8,128)(2,1)}, bf16[128,1024]{1,0:T(8,128)(2,1)S(1)}, u32[]{:S(2)}, u32[]{:S(2)}) collective-permute-start(bf16[128,1024]{1,0:T(8,128)(2,1)} %bitcast.81), channel_id=1, source_target_pairs={{0,2},{2,4},{4,6},{6,8},{8,10},{10,12},{12,14},{14,16},{16,18},{18... | collective-permute-start | bytes 786440 | tf_op jit(solution)/shard_map/ppermute | solution.py:18
  26.3 11.6 %collective-permute-start.2 = (bf16[128,1024]{1,0:T(8,128)(2,1)S(1)}, bf16[128,1024]{1,0:T(8,128)(2,1)S(1)}, u32[]{:S(2)}, u32[]{:S(2)}) collective-permute-start(bf16[128,1024]{1,0:T(8,128)(2,1)S(1)} %collective-permute-done.1), channel_id=1, source_target_pairs={{0,2},{2,4},{4,6},{6,8},{8,10},{10,12},{12,14},{14,16},{16,18},{18... | collective-permute-start | bytes 786440 | tf_op jit(solution)/shard_map/ppermute | solution.py:18
  37.9 13.5 %collective-permute-start.3 = (bf16[128,1024]{1,0:T(8,128)(2,1)S(1)}, bf16[128,1024]{1,0:T(8,128)(2,1)S(1)}, u32[]{:S(2)}, u32[]{:S(2)}) collective-permute-start(bf16[128,1024]{1,0:T(8,128)(2,1)S(1)} %collective-permute-done.2), channel_id=1, source_target_pairs={{0,2},{2,4},{4,6},{6,8},{8,10},{10,12},{12,14},{14,16},{16,18},{18... | collective-permute-start | bytes 786440 | tf_op jit(solution)/shard_map/ppermute | solution.py:18
  51.4 11.1 %collective-permute-start.4 = (bf16[128,1024]{1,0:T(8,128)(2,1)S(1)}, bf16[128,1024]{1,0:T(8,128)(2,1)S(1)}, u32[]{:S(2)}, u32[]{:S(2)}) collective-permute-start(bf16[128,1024]{1,0:T(8,128)(2,1)S(1)} %collective-permute-done.3), channel_id=1, source_target_pairs={{0,2},{2,4},{4,6},{6,8},{8,10},{10,12},{12,14},{14,16},{16,18},{18... | collective-permute-start | bytes 786440 | tf_op jit(solution)/shard_map/ppermute | solution.py:18
  110.9 16.8 %collective-permute-start.6 = (bf16[1024,3072]{1,0:T(8,128)(2,1)}, bf16[1024,3072]{1,0:T(8,128)(2,1)}, u32[]{:S(2)}, u32[]{:S(2)}) collective-permute-start(bf16[1024,3072]{1,0:T(8,128)(2,1)} %all-gather.2.cloned.1.call-done), channel_id=1, source_target_pairs={{0,1},{1,0},{2,3},{3,2},{4,5},{5,4},{6,7},{7,6},{8,9},{9,8},{10,11... | collective-permute-start | bytes 18874376 | tf_op jit(solution)/shard_map/ppermute | solution.py:78
  112.8 12.2 %collective-permute-start.5 = (bf16[5,128,1024]{2,1,0:T(8,128)(2,1)S(1)}, bf16[5,128,1024]{2,1,0:T(8,128)(2,1)S(1)}, u32[]{:S(2)}, u32[]{:S(2)}) collective-permute-start(bf16[5,128,1024]{2,1,0:T(8,128)(2,1)S(1)} %constant_dynamic-update-slice_fusion.2), channel_id=1, source_target_pairs={{0,1},{1,0},{2,3},{3,2},{4,5},{5,4},{6,7},{7,6},{8,9},{9,8},{10,11... | collective-permute-start | bytes 3932168 | tf_op jit(solution)/shard_map/ppermute | solution.py:84
  125.4 2.3 slice-start
  125.7 1.2 copy-start.6
  125.7 2.7 %slice-start.1 = ((s8[6291456]{0:T(1024)(128)(4,1)}), s8[2097152]{0:T(1024)(128)(4,1)S(1)}, s32[]{:S(2)}) async-start(s8[6291456]{0:T(1024)(128)(4,1)} %bitcast.74), calls=%async_computation.2 | async-start | bytes 4194304
  138.6 4.6 %copy-start = (bf16[1024,6144]{1,0:T(8,128)(2,1)}, bf16[1024,6144]{1,0:T(8,128)(2,1)S(1)}, u32[]{:S(2)}) copy-start(bf16[1024,6144]{1,0:T(8,128)(2,1)S(1)} %maximum_select_fusion) | copy-start | bytes 37748740
  176.5 2.4 copy-start.7
  178.6 3.3 %copy-start.2 = (bf16[128,1024]{1,0:T(8,128)(2,1)}, bf16[128,1024]{1,0:T(8,128)(2,1)S(1)}, u32[]{:S(2)}) copy-start(bf16[128,1024]{1,0:T(8,128)(2,1)S(1)} %get-tuple-element.120) | copy-start | bytes 786436
  178.9 10.9 %copy-start.3 = (f32[9,1024]{1,0:T(8,128)S(1)}, f32[9,1024]{1,0:T(8,128)}, u32[]{:S(2)}) copy-start(f32[9,1024]{1,0:T(8,128)} %param.19) | copy-start | bytes 110596
  178.9 60.5 %copy-start.4 = (f32[1024]{0:T(1024)S(1)}, f32[1024]{0:T(1024)}, u32[]{:S(2)}) copy-start(f32[1024]{0:T(1024)} %param.21) | copy-start | bytes 12292
  178.9 60.5 %copy-start.5 = (f32[1024]{0:T(1024)S(1)}, f32[1024]{0:T(1024)}, u32[]{:S(2)}) copy-start(f32[1024]{0:T(1024)} %param.20) | copy-start | bytes 12292
  182.1 9.0 %collective-permute-start.7 = (bf16[4,1024]{1,0:T(4,128)(2,1)S(1)}, bf16[4,1024]{1,0:T(4,128)(2,1)S(1)}, u32[]{:S(2)}, u32[]{:S(2)}) collective-permute-start(bf16[4,1024]{1,0:T(4,128)(2,1)S(1)} %get-tuple-element.104), channel_id=1, source_target_pairs={{0,1},{1,2},{2,3},{3,4},{4,5},{5,6},{6,7},{7,8},{8,9},{9,10},{10,1... | collective-permute-start | bytes 24584 | tf_op jit(solution)/shard_map/ppermute | solution.py:28
  184.2 7.0 %collective-permute-start.8 = (bf16[4,1024]{1,0:T(4,128)(2,1)S(1)}, bf16[4,1024]{1,0:T(4,128)(2,1)S(1)}, u32[]{:S(2)}, u32[]{:S(2)}) collective-permute-start(bf16[4,1024]{1,0:T(4,128)(2,1)S(1)} %get-tuple-element.105), channel_id=1, source_target_pairs={{1,0},{2,1},{3,2},{4,3},{5,4},{6,5},{7,6},{8,7},{9,8},{10,9},{11,1... | collective-permute-start | bytes 24584 | tf_op jit(solution)/shard_map/ppermute | solution.py:30
Sparse Core Ops, SparseCore 0:
  13.8 96.9 all-gather.1
where the time goes:
time: 248 us; the launch traced here: 247 us
  waiting for transfers between devices  96.9 us (39%)
  blocking collectives  47.5 us (19%)
  matrix products  26.3 us (11%)
  starting transfers between devices  23.2 us (9%)
  other arithmetic  19.3 us (8%)
  local copies, waits for them, and re-layouts  18.8 us (8%)
  between operations  15.2 us (6%)
    all_gather x1, waiting for transfers between devices, on_device(): lax.all_gather(pair.reshape(-1, half), ('x', 'y'), axis=0, tiled=True)  48.2 us
    psum x4, blocking collectives, on_device(): moments = lax.psum(moments, axis)  47.5 us
    ppermute x4, waiting for transfers between devices, passed_along(): lax.ppermute(value, axis, [(source, source + steps) for source in range(f...  39.6 us
    dot_general x4, matrix products, contract_with(): return jnp.dot(left, rows_piece, preferred_element_type=jnp.float32)  12.3 us
    select_n x1, other arithmetic, on_device(): jnp.where(core == 0, jnp.concatenate([gathered, other], axis=1), jnp.conc...  10.2 us
    ppermute x4, starting transfers between devices, passed_along(): lax.ppermute(value, axis, [(source, source + steps) for source in range(f...  9.21 us
    ppermute x1, waiting for transfers between devices, on_device(): theirs = lax.ppermute(mine, 'core', swap)  7.81 us
    dot_general x4, matrix products, attend_group(): jnp.einsum('hqk,khd->qhd', probs, value_part, preferred_element_type=jnp....  7 us
  transfers between devices with their start and end apart: 10, of which 7 were waited for; matrix products, arithmetic and copies ran while one was open for 2% of the time, Pallas kernels for 0%

commit v1 on v0

--- a/solution.py
+++ b/solution.py
@@ -65,7 +65,12 @@
     given = lax.ppermute(jnp.where(core == 0, halves[1], halves[0]), "core", swap)
     kept = jnp.where(core == 0, halves[0], halves[1])
     pair = jnp.where(core == 0, jnp.stack([kept, given]), jnp.stack([given, kept]))
-    gathered = lax.all_gather(pair.reshape(-1, half), ("x", "y"), axis=0, tiled=True)
+    gathered = jnp.concatenate(
+        lax.all_to_all(
+            jnp.stack([pair.reshape(-1, half)] * lax.axis_size(("x", "y"))), ("x", "y"), 0, 0
+        ),
+        axis=0,
+    )
     prior_blocks = LEFT // frame_count
     chip_hops = prior_blocks // cores
     blocks = [stream]

time: 248 us -> 337 us (1.36)
  waiting for transfers between devices: 96.9 us -> 177 us
  between operations: 15.2 us -> 1.75 us
  starting transfers between devices: 23.2 us -> 36.4 us
    ppermute x4, waiting for transfers between devices: 39.6 us -> 168 us  [passed_along(): lax.ppermute(value, axis, [(source, source + steps) for source in range(f...]
    all_gather x1 -> x0, waiting for transfers between devices: 48.2 us -> none  [on_device(): lax.all_gather(pair.reshape(-1, half), ('x', 'y'), axis=0, tiled=True)]
    all_to_all x0 -> x1, starting transfers between devices: none -> 10.5 us  [on_device(): lax.all_to_all(jnp.stack([pair.reshape(-1, half)] * lax.axis_size(('x', '...]
    select_n x1, other arithmetic: 10.2 us -> 13.9 us  [on_device(): jnp.where(core == 0, jnp.concatenate([gathered, other], axis=1), jnp.conc...]
    another operation x0 -> x1, local copies, waits for them, and re-layouts: none -> 3.44 us  [on_device(): jnp.stack([pair.reshape(-1, half)] * lax.axis_size(('x', 'y')))]
  transfers between devices with their start and end apart: 10 -> 10, of which waited for: 7 -> 6; matrix products, arithmetic and copies ran while one was open for 2% -> 2% of each run, Pallas kernels for 0% -> 0%
where the time goes in v1:
time: 337 us; the launch traced here: 336 us
  waiting for transfers between devices  177 us (53%)
  blocking collectives  50.6 us (15%)
  starting transfers between devices  36.4 us (11%)
  matrix products  26.3 us (8%)
  other arithmetic  22.4 us (7%)
  local copies, waits for them, and re-layouts  21.5 us (6%)
    ppermute x4, waiting for transfers between devices, passed_along(): lax.ppermute(value, axis, [(source, source + steps) for source in range(f...  168 us
    psum x4, blocking collectives, on_device(): moments = lax.psum(moments, axis)  50.6 us
    select_n x1, other arithmetic, on_device(): jnp.where(core == 0, jnp.concatenate([gathered, other], axis=1), jnp.conc...  13.9 us
    dot_general x4, matrix products, contract_with(): return jnp.dot(left, rows_piece, preferred_element_type=jnp.float32)  12.3 us
    ppermute x4, starting transfers between devices, passed_along(): lax.ppermute(value, axis, [(source, source + steps) for source in range(f...  11.9 us
    all_to_all x1, starting transfers between devices, on_device(): lax.all_to_all(jnp.stack([pair.reshape(-1, half)] * lax.axis_size(('x', '...  10.5 us
    ppermute x1, waiting for transfers between devices, on_device(): theirs = lax.ppermute(mine, 'core', swap)  7.81 us
    dot_general x4, matrix products, attend_group(): jnp.einsum('hqk,khd->qhd', probs, value_part, preferred_element_type=jnp....  7 us
  transfers between devices with their start and end apart: 10, of which 6 were waited for; matrix products, arithmetic and copies ran while one was open for 2% of the time, Pallas kernels for 0%

profile of v1, /device:TPU:2, one launch (start us, length us, event | category | flops | bytes accessed | tf_op | source)
XLA Modules:
  0.0 335.7 jit_solution(2539460636289066436)
XLA Ops:
  0.6 0.8 constant_dynamic-update-slice_fusion.1
  1.4 0.8 constant_dynamic-update-slice_fusion
  2.2 0.9 select_bitcast_fusion
  3.2 1.9 collective-permute-start
  5.1 1.3 collective-permute-done
  6.4 3.4 %stack.50 = bf16[32,32,3072]{2,1,0:T(8,128)(2,1)} broadcast(bf16[32,3072]{1,0:T(8,128)(2,1)S(1)} %bitcast.79), dimensions={1,2} | broadcast | bytes 6488064 | tf_op jit(solution)/shard_map/stack | solution.py:70
  9.8 10.5 %all-to-all-start = ((bf16[32,32,3072]{2,1,0:T(8,128)(2,1)}), bf16[32,32,3072]{2,1,0:T(8,128)(2,1)}, u32[]{:S(2)}, u32[]{:S(2)}) async-start(bf16[32,32,3072]{2,1,0:T(8,128)(2,1)} %stack.50), calls=%async_computation | async-start | bytes 12582912 | tf_op jit(solution)/shard_map/all_to_all | solution.py:69
  20.4 0.0 copy-start.8
  20.4 3.4 %collective-permute-start.1 = (bf16[128,1024]{1,0:T(8,128)(2,1)S(1)}, bf16[128,1024]{1,0:T(8,128)(2,1)S(1)}, u32[]{:S(2)}, u32[]{:S(2)}) collective-permute-start(bf16[128,1024]{1,0:T(8,128)(2,1)S(1)} %bitcast.80), channel_id=1, source_target_pairs={{0,2},{2,4},{4,6},{6,8},{8,10},{10,12},{12,14},{14,16},{16,18},{18... | collective-permute-start | bytes 786440 | tf_op jit(solution)/shard_map/ppermute | solution.py:18
  23.8 143.7 %collective-permute-done.1 = bf16[128,1024]{1,0:T(8,128)(2,1)S(1)} collective-permute-done((bf16[128,1024]{1,0:T(8,128)(2,1)S(1)}, bf16[128,1024]{1,0:T(8,128)(2,1)S(1)}, u32[]{:S(2)}, u32[]{:S(2)}) %collective-permute-start.1) | collective-permute-done | bytes 262176 | tf_op jit(solution)/shard_map/ppermute | solution.py:18
  167.5 4.4 %collective-permute-start.2 = (bf16[128,1024]{1,0:T(8,128)(2,1)S(1)}, bf16[128,1024]{1,0:T(8,128)(2,1)S(1)}, u32[]{:S(2)}, u32[]{:S(2)}) collective-permute-start(bf16[128,1024]{1,0:T(8,128)(2,1)S(1)} %collective-permute-done.1), channel_id=1, source_target_pairs={{0,2},{2,4},{4,6},{6,8},{8,10},{10,12},{12,14},{14,16},{16,18},{18... | collective-permute-start | bytes 786440 | tf_op jit(solution)/shard_map/ppermute | solution.py:18
  171.8 7.1 %collective-permute-done.2 = bf16[128,1024]{1,0:T(8,128)(2,1)S(1)} collective-permute-done((bf16[128,1024]{1,0:T(8,128)(2,1)S(1)}, bf16[128,1024]{1,0:T(8,128)(2,1)S(1)}, u32[]{:S(2)}, u32[]{:S(2)}) %collective-permute-start.2) | collective-permute-done | bytes 262176 | tf_op jit(solution)/shard_map/ppermute | solution.py:18
  179.0 2.3 collective-permute-start.3
  181.2 8.4 %collective-permute-done.3 = bf16[128,1024]{1,0:T(8,128)(2,1)S(1)} collective-permute-done((bf16[128,1024]{1,0:T(8,128)(2,1)S(1)}, bf16[128,1024]{1,0:T(8,128)(2,1)S(1)}, u32[]{:S(2)}, u32[]{:S(2)}) %collective-permute-start.3) | collective-permute-done | bytes 262176 | tf_op jit(solution)/shard_map/ppermute | solution.py:18
  189.6 1.9 collective-permute-start.4
  191.5 8.4 %collective-permute-done.4 = bf16[128,1024]{1,0:T(8,128)(2,1)S(1)} collective-permute-done((bf16[128,1024]{1,0:T(8,128)(2,1)S(1)}, bf16[128,1024]{1,0:T(8,128)(2,1)S(1)}, u32[]{:S(2)}, u32[]{:S(2)}) %collective-permute-start.4) | collective-permute-done | bytes 262176 | tf_op jit(solution)/shard_map/ppermute | solution.py:18
  200.1 1.9 collective-permute-start.6
  202.0 2.4 collective-permute-start.5
  204.5 0.6 dynamic_slice.18
  205.1 0.7 broadcast_compare_fusion
  205.8 0.7 fusion.66
  206.4 7.8 %collective-permute-done.5 = bf16[5,128,1024]{2,1,0:T(8,128)(2,1)S(1)} collective-permute-done((bf16[5,128,1024]{2,1,0:T(8,128)(2,1)S(1)}, bf16[5,128,1024]{2,1,0:T(8,128)(2,1)S(1)}, u32[]{:S(2)}, u32[]{:S(2)}) %collective-permute-start.5) | collective-permute-done | bytes 1310752 | tf_op jit(solution)/shard_map/ppermute | solution.py:89
  214.2 0.4 maximum_select_fusion.1
  214.7 0.2 copy.15
  214.9 0.0 copy-start.6
  214.9 0.4 convert_reduce_fusion
  215.3 0.8 fusion.20
  216.1 0.8 fusion.22
  216.9 13.9 %maximum_select_fusion = bf16[1024,6144]{1,0:T(8,128)(2,1)S(1)} fusion(bf16[1024,3072]{1,0:T(8,128)(2,1)} %collective-permute-done.6, bf16[1024,3072]{1,0:T(8,128)(2,1)} %bitcast.5, pred[]{:T(512)S(6)} %eq.6), kind=kLoop, calls=%fused_computation.20 | loop fusion | flops 56623104 | bytes 25165824 | tf_op jit(solution)/shard_map/jit(_where)/select_n | solution.py:84
  230.8 0.4 fusion.39
  231.3 4.1 %copy-done = bf16[1024,6144]{1,0:T(8,128)(2,1)} copy-done((bf16[1024,6144]{1,0:T(8,128)(2,1)}, bf16[1024,6144]{1,0:T(8,128)(2,1)S(1)}, u32[]{:S(2)}) %copy-start) | copy-done | bytes 12582936
  235.4 6.7 %convolution_convert_fusion = bf16[1152,2048]{1,0:T(8,128)(2,1)} fusion(bf16[1152,1024]{1,0:T(8,128)(2,1)S(1)} %fusion.22, bf16[1024,6144]{1,0:T(8,128)(2,1)S(1)} %maximum_select_fusion), kind=kOutput, calls=%fused_computation.21 | convolution fusion | flops 4834197504 | bytes 11272192 | tf_op jit(solution)/shard_map/dot_general | solution.py:44
  242.1 0.2 copy.17
  242.3 4.3 %fusion.69 = (bf16[1152,1024]{1,0:T(8,128)(2,1)S(1)}, bf16[1152,1024]{1,0:T(8,128)(2,1)}) fusion(bf16[1152,2048]{1,0:T(8,128)(2,1)} %convolution_convert_fusion), kind=kLoop, calls=%fused_computation.109 | loop fusion | bytes 9437184 | tf_op jit(solution)/shard_map/slice | solution.py:100
  246.6 4.3 %copy.16 = bf16[1152,1024]{0,1:T(8,128)(2,1)} copy(bf16[1152,1024]{1,0:T(8,128)(2,1)} %get-tuple-element.103) | data formatting | bytes 4718592 | tf_op jit(solution)/shard_map/slice | solution.py:101
  250.9 2.6 copy.18
  253.5 15.3 %while.11 = (s32[]{:T(128)}, bf16[4,128,4,64]{1,3,2,0:T(8,128)(2,1)S(1)}, bf16[4,1152,4,64]{1,3,2,0:T(8,128)(2,1)}, bf16[4,128,4,64]{1,3,2,0:T(8,128)(2,1)S(1)},...) while((s32[]{:T(128)}, ...), condition=%wide.region_4.5_spmd.clone, body=%wide.region_2.4_spmd.clone.sunk | while | flops 154420864 | bytes 8694133 | solution.py:129
  253.5 0.3 or_and_fusion.2
  253.8 1.7 fusion.85
  255.5 1.7 fusion.86
  257.3 0.3 or_and_fusion.2
  257.6 1.7 fusion.85
  259.3 1.8 fusion.86
  261.1 0.3 or_and_fusion.2
  261.4 1.7 fusion.85
  263.2 1.8 fusion.86
  264.9 0.3 or_and_fusion.2
  265.2 1.7 fusion.85
  267.0 1.7 fusion.86
  268.8 0.0 copy-start.7
  268.8 2.2 convert_reduce_fusion.1
  270.9 0.2 fusion.44
  271.2 0.0 copy-start.5
  271.2 3.0 fusion.23
  274.2 0.2 fusion.53
  274.4 2.0 collective-permute-start.7
  276.5 5.6 %collective-permute-start.8 = (bf16[4,1024]{1,0:T(4,128)(2,1)S(1)}, bf16[4,1024]{1,0:T(4,128)(2,1)S(1)}, u32[]{:S(2)}, u32[]{:S(2)}) collective-permute-start(bf16[4,1024]{1,0:T(4,128)(2,1)S(1)} %get-tuple-element.105), channel_id=1, source_target_pairs={{1,0},{2,1},{3,2},{4,3},{5,4},{6,5},{7,6},{8,7},{9,8},{10,9},{11,1... | collective-permute-start | bytes 24584 | tf_op jit(solution)/shard_map/ppermute | solution.py:30
  282.2 0.6 reduce_sum.77
  283.5 0.7 select_reduce_fusion
  284.2 2.5 all-reduce.3
  286.6 19.4 %all-reduce = (f32[1024]{0:T(1024)S(1)}, f32[1024]{0:T(1024)S(1)}) all-reduce(f32[1024]{0:T(1024)S(1)} %get-tuple-element.99, f32[1024]{0:T(1024)S(1)} %get-tuple-element.100), channel_id=1, replica_groups=mesh['call'=8,'x'=4,'y'=8,'core'=2] {'y'}, use_global_device_ids=true, to_apply=%region_15.16 | all-reduce | flops 2048 | bytes 16384 | tf_op jit(solution)/shard_map/psum | solution.py:149
  306.0 7.3 %all-reduce.2 = (f32[1024]{0:T(1024)S(1)}, f32[1024]{0:T(1024)S(1)}) all-reduce(f32[1024]{0:T(1024)S(1)} %get-tuple-element.93, f32[1024]{0:T(1024)S(1)} %get-tuple-element.94), channel_id=1, replica_groups=mesh['call'=8,'x'=4,'y'=8,'core'=2] {'x'}, use_global_device_ids=true, to_apply=%region_16.17 | all-reduce | flops 2048 | bytes 16384 | tf_op jit(solution)/shard_map/psum | solution.py:149
  313.3 21.4 %all-reduce.1 = (f32[1024]{0:T(1024)S(1)}, f32[1024]{0:T(1024)S(1)}) all-reduce(f32[1024]{0:T(1024)S(1)} %get-tuple-element.97, f32[1024]{0:T(1024)S(1)} %get-tuple-element.98), channel_id=1, replica_groups=mesh['call'=8,'x'=4,'y'=8,'core'=2] {'call'}, use_global_device_ids=true, to_apply=%region_17.18 | all-reduce | flops 2048 | bytes 16384 | tf_op jit(solution)/shard_map/psum | solution.py:149
  334.8 0.9 fusion.65
  (34 shorter events, 0.3 us)
Async XLA Ops:
  3.2 3.2 collective-permute-start
  9.8 10.6 %copy-start.1 = (bf16[1,128,1024]{2,1,0:T(8,128)(2,1)S(1)}, bf16[1,128,1024]{2,1,0:T(8,128)(2,1)}, u32[]{:S(2)}) copy-start(bf16[1,128,1024]{2,1,0:T(8,128)(2,1)} %param.12) | copy-start | bytes 786436
  9.8 190.3 %all-to-all-start = ((bf16[32,32,3072]{2,1,0:T(8,128)(2,1)}), bf16[32,32,3072]{2,1,0:T(8,128)(2,1)}, u32[]{:S(2)}, u32[]{:S(2)}) async-start(bf16[32,32,3072]{2,1,0:T(8,128)(2,1)} %stack.50), calls=%async_computation | async-start | bytes 12582912 | tf_op jit(solution)/shard_map/all_to_all | solution.py:69
  20.4 184.1 %copy-start.8 = (s32[8]{0:T(128)S(1)}, s32[8]{0:T(128)}, u32[]{:S(2)}) copy-start(s32[8]{0:T(128)} %param.13) | copy-start | bytes 100
  20.4 147.1 %collective-permute-start.1 = (bf16[128,1024]{1,0:T(8,128)(2,1)S(1)}, bf16[128,1024]{1,0:T(8,128)(2,1)S(1)}, u32[]{:S(2)}, u32[]{:S(2)}) collective-permute-start(bf16[128,1024]{1,0:T(8,128)(2,1)S(1)} %bitcast.80), channel_id=1, source_target_pairs={{0,2},{2,4},{4,6},{6,8},{8,10},{10,12},{12,14},{14,16},{16,18},{18... | collective-permute-start | bytes 786440 | tf_op jit(solution)/shard_map/ppermute | solution.py:18
  167.5 11.5 %collective-permute-start.2 = (bf16[128,1024]{1,0:T(8,128)(2,1)S(1)}, bf16[128,1024]{1,0:T(8,128)(2,1)S(1)}, u32[]{:S(2)}, u32[]{:S(2)}) collective-permute-start(bf16[128,1024]{1,0:T(8,128)(2,1)S(1)} %collective-permute-done.1), channel_id=1, source_target_pairs={{0,2},{2,4},{4,6},{6,8},{8,10},{10,12},{12,14},{14,16},{16,18},{18... | collective-permute-start | bytes 786440 | tf_op jit(solution)/shard_map/ppermute | solution.py:18
  179.0 10.6 %collective-permute-start.3 = (bf16[128,1024]{1,0:T(8,128)(2,1)S(1)}, bf16[128,1024]{1,0:T(8,128)(2,1)S(1)}, u32[]{:S(2)}, u32[]{:S(2)}) collective-permute-start(bf16[128,1024]{1,0:T(8,128)(2,1)S(1)} %collective-permute-done.2), channel_id=1, source_target_pairs={{0,2},{2,4},{4,6},{6,8},{8,10},{10,12},{12,14},{14,16},{16,18},{18... | collective-permute-start | bytes 786440 | tf_op jit(solution)/shard_map/ppermute | solution.py:18
  189.6 10.4 %collective-permute-start.4 = (bf16[128,1024]{1,0:T(8,128)(2,1)S(1)}, bf16[128,1024]{1,0:T(8,128)(2,1)S(1)}, u32[]{:S(2)}, u32[]{:S(2)}) collective-permute-start(bf16[128,1024]{1,0:T(8,128)(2,1)S(1)} %collective-permute-done.3), channel_id=1, source_target_pairs={{0,2},{2,4},{4,6},{6,8},{8,10},{10,12},{12,14},{14,16},{16,18},{18... | collective-permute-start | bytes 786440 | tf_op jit(solution)/shard_map/ppermute | solution.py:18
  200.1 16.8 %collective-permute-start.6 = (bf16[1024,3072]{1,0:T(8,128)(2,1)}, bf16[1024,3072]{1,0:T(8,128)(2,1)}, u32[]{:S(2)}, u32[]{:S(2)}) collective-permute-start(bf16[1024,3072]{1,0:T(8,128)(2,1)} %bitcast.5), channel_id=1, source_target_pairs={{0,1},{1,0},{2,3},{3,2},{4,5},{5,4},{6,7},{7,6},{8,9},{9,8},{10,11... | collective-permute-start | bytes 18874376 | tf_op jit(solution)/shard_map/ppermute | solution.py:83
  202.0 12.2 %collective-permute-start.5 = (bf16[5,128,1024]{2,1,0:T(8,128)(2,1)S(1)}, bf16[5,128,1024]{2,1,0:T(8,128)(2,1)S(1)}, u32[]{:S(2)}, u32[]{:S(2)}) collective-permute-start(bf16[5,128,1024]{2,1,0:T(8,128)(2,1)S(1)} %constant_dynamic-update-slice_fusion.2), channel_id=1, source_target_pairs={{0,1},{1,0},{2,3},{3,2},{4,5},{5,4},{6,7},{7,6},{8,9},{9,8},{10,11... | collective-permute-start | bytes 3932168 | tf_op jit(solution)/shard_map/ppermute | solution.py:89
  214.9 1.2 copy-start.6
  230.8 4.6 %copy-start = (bf16[1024,6144]{1,0:T(8,128)(2,1)}, bf16[1024,6144]{1,0:T(8,128)(2,1)S(1)}, u32[]{:S(2)}) copy-start(bf16[1024,6144]{1,0:T(8,128)(2,1)S(1)} %maximum_select_fusion) | copy-start | bytes 37748740
  268.8 2.4 copy-start.7
  270.9 3.3 copy-start.2
  271.2 10.9 %copy-start.3 = (f32[9,1024]{1,0:T(8,128)S(1)}, f32[9,1024]{1,0:T(8,128)}, u32[]{:S(2)}) copy-start(f32[9,1024]{1,0:T(8,128)} %param.19) | copy-start | bytes 110596
  271.2 63.6 %copy-start.4 = (f32[1024]{0:T(1024)S(1)}, f32[1024]{0:T(1024)}, u32[]{:S(2)}) copy-start(f32[1024]{0:T(1024)} %param.21) | copy-start | bytes 12292
  271.2 63.6 %copy-start.5 = (f32[1024]{0:T(1024)S(1)}, f32[1024]{0:T(1024)}, u32[]{:S(2)}) copy-start(f32[1024]{0:T(1024)} %param.20) | copy-start | bytes 12292
  274.4 9.0 %collective-permute-start.7 = (bf16[4,1024]{1,0:T(4,128)(2,1)S(1)}, bf16[4,1024]{1,0:T(4,128)(2,1)S(1)}, u32[]{:S(2)}, u32[]{:S(2)}) collective-permute-start(bf16[4,1024]{1,0:T(4,128)(2,1)S(1)} %get-tuple-element.104), channel_id=1, source_target_pairs={{0,1},{1,2},{2,3},{3,4},{4,5},{5,6},{6,7},{7,8},{8,9},{9,10},{10,1... | collective-permute-start | bytes 24584 | tf_op jit(solution)/shard_map/ppermute | solution.py:28
  276.5 7.0 %collective-permute-start.8 = (bf16[4,1024]{1,0:T(4,128)(2,1)S(1)}, bf16[4,1024]{1,0:T(4,128)(2,1)S(1)}, u32[]{:S(2)}, u32[]{:S(2)}) collective-permute-start(bf16[4,1024]{1,0:T(4,128)(2,1)S(1)} %get-tuple-element.105), channel_id=1, source_target_pairs={{1,0},{2,1},{3,2},{4,3},{5,4},{6,5},{7,6},{8,7},{9,8},{10,9},{11,1... | collective-permute-start | bytes 24584 | tf_op jit(solution)/shard_map/ppermute | solution.py:30
